TPU v7x, 512 devices: a whole 4x8x8 slice. The times are simulated.
512 devices in a mesh: dp: 16 (over x_lo, y), space: 32 (over x_hi, z, core).
Axes of the slice: x: 4 (x_hi: 2, x_lo: 2; x = x_hi * 2 + x_lo), y: 8, z: 8, core: 2. Of those that a mesh axis runs over, the one named last changes fastest.
Arguments:
- inputs: bfloat16 [16, 10, 64, 32, 128], P('dp', None, 'space'), may hold values from -8 to 8
- land_mask: int32 [16, 10, 64, 32], P('dp', None, 'space'), may hold values 0 or 1
- weight_one: float32 [128, 27, 128], P('dp'), may hold values from -0.109375 to 0.109375
- weight_two: float32 [128, 27, 128], P('dp'), may hold values from -0.109375 to 0.109375
- cotangent: bfloat16 [16, 10, 64, 32, 128], P('dp', None, 'space'), may hold values from -6 to 6
Outputs:
- prediction: bfloat16 [16, 10, 64, 32, 128], P('dp', None, 'space')
- input_grad: bfloat16 [16, 10, 64, 32, 128], P('dp', None, 'space')
- grad_one: float32 [128, 27, 128], P('dp')
- grad_two: float32 [128, 27, 128], P('dp')
All inputs are finite; a program needn't handle non-finite values. No bound on the sum of `land_mask` on one device may be relied on, other than what follows from the above.
Results may differ from a plain program's by a relative error of at most 0.0067.
Values may be sent and summed in bfloat16 or wider, within the bound.
No kernel may reach another device: no remote copies, remote signals or barrier semaphores. Data moves between devices by JAX's collectives and lax.ppermute only.
A program may use at most 64 MiB of HBM per device.

v0:
```python
import jax
import jax.numpy as jnp
from jax import lax
from jax.sharding import PartitionSpec as P

HALO = 2
SPATIAL = ("NDHWC", "DHWIO", "NDHWC")


def exchange_rows(cells, width):
    count = lax.axis_size("space")
    ends = count - 1
    rows = cells.shape[2]
    head = lax.slice_in_dim(cells, 0, width, axis=2)
    tail = lax.slice_in_dim(cells, rows - width, rows, axis=2)
    above = lax.ppermute(tail, "space", [(i, i + 1) for i in range(ends)])
    below = lax.ppermute(head, "space", [(i + 1, i) for i in range(ends)])
    return jnp.concatenate([above, cells, below], axis=2)


def pad_depth_cols(field):
    return jnp.pad(field, ((0, 0), (1, 1), (0, 0), (1, 1), (0, 0)))


def conv(padded, kernel):
    return lax.conv_general_dilated(
        padded, kernel, (1, 1, 1), "VALID", dimension_numbers=SPATIAL,
        preferred_element_type=jnp.float32,
    )


def weight_grad(padded, back):
    out = lax.conv_general_dilated(
        padded, back, (1, 1, 1), "VALID", dimension_numbers=("CDHWN", "IDHWO", "NDHWC"),
        preferred_element_type=jnp.float32,
    )
    return out.reshape(out.shape[0], 27, out.shape[4])


def gather_kernel(weight, issued=None):
    count = lax.axis_size("dp")
    local = weight.astype(jnp.bfloat16)
    copies = jnp.broadcast_to(local[None], (count,) + local.shape)
    if issued is not None:
        copies, issued = lax.optimization_barrier((copies, issued))
    full = lax.all_to_all(copies, "dp", 0, 0).reshape((-1,) + local.shape[1:])
    channel = full.shape[0]
    forward = jnp.transpose(full.reshape(channel, 3, 3, 3, full.shape[2]), (1, 2, 3, 0, 4))
    backward = jnp.transpose(forward[::-1, ::-1, ::-1], (0, 1, 2, 4, 3))
    if issued is not None:
        return forward, backward, issued
    return forward, backward


def reduce_grads(grads):
    count = lax.axis_size("dp")
    size = lax.axis_size("space")
    me = lax.axis_index("space")
    core = me % 2
    rows = grads[0].shape[0] // count
    parts = jnp.stack([g.reshape((count, 2, rows // 2) + g.shape[1:]) for g in grads], axis=1)
    keep = lax.dynamic_index_in_dim(parts, core, axis=2, keepdims=False)
    send = lax.dynamic_index_in_dim(parts, 1 - core, axis=2, keepdims=False)
    mine = keep + lax.ppermute(send, "space", [(i, i ^ 1) for i in range(size)])
    owned = lax.all_to_all(mine.astype(jnp.bfloat16), "dp", 0, 0).astype(jnp.float32).sum(axis=0)
    pairs = size // 2
    pieces = owned.reshape(pairs, -1)
    spread = jnp.repeat(pieces, 2, axis=0)
    got = lax.all_to_all(spread, "space", 0, 0).reshape(pairs, 2, -1)
    piece = lax.dynamic_index_in_dim(got, core, axis=1, keepdims=False).sum(axis=0)
    copies = jnp.broadcast_to(piece[None], (size,) + piece.shape)
    full = lax.all_to_all(copies, "space", 0, 0).reshape(pairs, 2, -1)
    halves = jnp.transpose(full, (1, 0, 2)).reshape((2,) + owned.shape)
    joined = jnp.transpose(halves, (1, 0, 2, 3, 4)).reshape((len(grads), rows) + grads[0].shape[1:])
    return [joined[i] for i in range(len(grads))]


def on_device(inputs, land_mask, weight_one, weight_two, cotangent):
    rows = inputs.shape[2]
    channel = inputs.shape[4]
    mask = land_mask.astype(jnp.bfloat16)[..., None]
    back_two = (cotangent.astype(jnp.float32) * mask.astype(jnp.float32)).astype(jnp.bfloat16)
    k1, k1_t, (rimmed, mask) = gather_kernel(weight_one, (jnp.concatenate([inputs, back_two], axis=4), mask))
    both = exchange_rows(rimmed, HALO)
    mask_wide = exchange_rows(mask, HALO).astype(jnp.float32)
    in_wide = both[..., :channel]
    back_two_wide = both[..., channel:]
    mask_mid = mask_wide[:, :, 1 : rows + 3]
    mask_own = mask_wide[:, :, 2 : rows + 2]

    k2, k2_t = gather_kernel(weight_two)

    pre_one = conv(pad_depth_cols(in_wide), k1)
    sigma = jax.nn.sigmoid(pre_one)
    act_one = (mask_mid * (pre_one * sigma)).astype(jnp.bfloat16)
    act_pad = pad_depth_cols(act_one)
    prediction = (mask_own * conv(act_pad, k2)).astype(jnp.bfloat16)

    back_own = back_two_wide[:, :, HALO : HALO + rows]
    grad_two_terms = weight_grad(act_pad, back_own)
    grad_two_terms, back_two_wide = lax.optimization_barrier((grad_two_terms, back_two_wide))

    pull_one = conv(pad_depth_cols(back_two_wide), k2_t)
    back_one = (pull_one * mask_mid * sigma * (1.0 + pre_one * (1.0 - sigma))).astype(jnp.bfloat16)
    in_mid = pad_depth_cols(in_wide[:, :, 1 : rows + 3])
    grad_one_terms = weight_grad(in_mid, back_one[:, :, 1 : rows + 1])
    grad_one, grad_two = reduce_grads([grad_one_terms, grad_two_terms])
    input_grad = conv(pad_depth_cols(back_one), k1_t).astype(jnp.bfloat16)
    return (prediction, input_grad, grad_one, grad_two)


def solution(mesh):
    in_specs = (
        P("dp", None, "space", None, None),
        P("dp", None, "space", None),
        P("dp", None, None),
        P("dp", None, None),
        P("dp", None, "space", None, None),
    )
    out_specs = (
        P("dp", None, "space", None, None),
        P("dp", None, "space", None, None),
        P("dp", None, None),
        P("dp", None, None),
    )
    return jax.shard_map(
        on_device, mesh=mesh, in_specs=in_specs, out_specs=out_specs, check_vma=False
    )
```

profile of v0, /device:TPU:1, one launch (start us, length us, event | category | flops | bytes accessed | tf_op | source)
XLA Modules:
  0.0 163.3 jit_solution(2136099323514866574)
XLA Ops:
  0.6 0.7 convert_bitcast_fusion.2
  1.3 0.9 convert_element_type.62
  2.3 1.1 multiply_convert_fusion
  3.3 1.0 pad_maximum_fusion
  4.3 1.0 broadcast_in_dim.10
  5.4 8.7 %all-to-all-start = ((bf16[16,8,27,128]{3,1,2,0:T(8,128)(2,1)}), bf16[16,8,27,128]{3,1,2,0:T(8,128)(2,1)S(1)}, u32[]{:S(2)}, u32[]{:S(2)}) async-start(bf16[16,8,27,128]{3,1,2,0:T(8,128)(2,1)} %broadcast_in_dim.10), calls=%async_computation | async-start | bytes 1769472 | tf_op jit(solution)/shard_map/all_to_all | solution.py:46
  14.1 4.8 %collective-permute-start.2 = (bf16[1,10,2,32,256]{4,3,2,1,0:T(8,128)(2,1)S(1)}, bf16[1,10,2,32,256]{4,3,2,1,0:T(8,128)(2,1)S(1)}, u32[]{:S(2)}, u32[]{:S(2)}) collective-permute-start(bf16[1,10,2,32,256]{4,3,2,1,0:T(8,128)(2,1)S(1)} %pad_maximum_fusion), channel_id=1, source_target_pairs={{0,1},{1,2},{2,3},{3,4},{4,5},{5,6},{6,7},{7,8},{8,9},{9,10},{10,1... | collective-permute-start | bytes 983048 | tf_op jit(solution)/shard_map/ppermute | solution.py:16
  18.9 1.9 %collective-permute-start.1 = (bf16[1,10,2,32,1]{3,2,1,4,0:T(2,128)(2,1)S(1)}, bf16[1,10,2,32,1]{3,2,1,4,0:T(2,128)(2,1)S(1)}, u32[]{:S(2)}, u32[]{:S(2)}) collective-permute-start(bf16[1,10,2,32,1]{3,2,1,4,0:T(2,128)(2,1)S(1)} %get-tuple-element.9), channel_id=1, source_target_pairs={{1,0},{2,1},{3,2},{4,3},{5,4},{6,5},{7,6},{8,7},{9,8},{10,9},{11,1... | collective-permute-start | bytes 3848 | tf_op jit(solution)/shard_map/ppermute | solution.py:17
  20.8 3.6 %collective-permute-start = (bf16[1,10,2,32,1]{3,2,1,4,0:T(2,128)(2,1)S(1)}, bf16[1,10,2,32,1]{3,2,1,4,0:T(2,128)(2,1)S(1)}, u32[]{:S(2)}, u32[]{:S(2)}) collective-permute-start(bf16[1,10,2,32,1]{3,2,1,4,0:T(2,128)(2,1)S(1)} %get-tuple-element.9), channel_id=1, source_target_pairs={{0,1},{1,2},{2,3},{3,4},{4,5},{5,6},{6,7},{7,8},{8,9},{9,10},{10,1... | collective-permute-start | bytes 3848 | tf_op jit(solution)/shard_map/ppermute | solution.py:16
  24.5 1.9 %collective-permute-start.3 = (bf16[1,10,2,32,256]{4,3,2,1,0:T(8,128)(2,1)S(1)}, bf16[1,10,2,32,256]{4,3,2,1,0:T(8,128)(2,1)S(1)}, u32[]{:S(2)}, u32[]{:S(2)}) collective-permute-start(bf16[1,10,2,32,256]{4,3,2,1,0:T(8,128)(2,1)S(1)} %pad_maximum_fusion), channel_id=1, source_target_pairs={{1,0},{2,1},{3,2},{4,3},{5,4},{6,5},{7,6},{8,7},{9,8},{10,9},{11,1... | collective-permute-start | bytes 983048 | tf_op jit(solution)/shard_map/ppermute | solution.py:17
  26.4 0.7 slice.35
  27.5 5.7 %collective-permute-done.3 = bf16[1,10,2,32,256]{4,3,2,1,0:T(8,128)(2,1)S(1)} collective-permute-done((bf16[1,10,2,32,256]{4,3,2,1,0:T(8,128)(2,1)S(1)}, bf16[1,10,2,32,256]{4,3,2,1,0:T(8,128)(2,1)S(1)}, u32[]{:S(2)}, u32[]{:S(2)}) %collective-permute-start.3) | collective-permute-done | bytes 327712 | tf_op jit(solution)/shard_map/ppermute | solution.py:17
  33.2 0.8 slice.63
  34.0 0.3 fusion.59
  34.3 0.2 copy.148
  34.5 0.2 pad.7.clone
  34.9 1.0 broadcast_in_dim.12
  35.9 8.1 %all-to-all-start.1 = ((bf16[16,8,27,128]{3,1,2,0:T(8,128)(2,1)}), bf16[16,8,27,128]{3,1,2,0:T(8,128)(2,1)S(1)}, u32[]{:S(2)}, u32[]{:S(2)}) async-start(bf16[16,8,27,128]{3,1,2,0:T(8,128)(2,1)} %broadcast_in_dim.12), calls=%async_computation.1 | async-start | bytes 1769472 | tf_op jit(solution)/shard_map/all_to_all | solution.py:46
  44.0 0.2 copy.112
  44.3 3.3 %add_divide_fusion = (f32[10,4,8,5,128]{4,2,3,1,0:T(8,128)S(1)}, f32[10,4,8,5,128]{4,2,3,1,0:T(8,128)S(1)}, f32[10,4,8,5,128]{4,2,3,1,0:T(8,128)S(1)}) fusion(bf16[128,3,3,3,128]{4,0,3,2,1:T(8,128)(2,1)S(1)} %bitcast.80, bf16[10,6,1,7,2,128]{5,3,4,1,0,2:T(8,128)(2,1)S(1)} %slice.52, bf16[10,6,1,8,5,128]{5,3,4,1,0,2:T(8,128)(2,1)S(1)} %copy.111, ...), kind=kOutput, calls=%fused_computation.32 | convolution fusion | flops 1325424640 | bytes 4171816 | tf_op jit(solution)/shard_map/conv_general_dilated | solution.py:26
  47.6 0.2 copy.113
  47.8 0.9 copy-done
  48.7 0.4 fusion.65
  49.1 5.8 %fusion.24 = f32[128,3,3,3,128]{4,0,3,2,1:T(8,128)} fusion(bf16[1,10,4,32,128]{4,2,3,1,0:T(4,128)(2,1)S(1)} %fusion.65, bf16[1,10,2,32,128]{4,3,2,1,0:T(8,128)(2,1)S(1)} %copy-done.9), kind=kOutput, calls=%fused_computation.41 | convolution fusion | flops 517472256 | bytes 2260992 | tf_op jit(solution)/shard_map/conv_general_dilated | solution.py:33
  54.9 0.2 copy.124
  55.1 0.2 copy.125
  55.3 0.2 copy.149
  55.6 0.2 pad.11.clone
  55.8 0.8 slice.57
  56.6 8.8 %all-to-all-done.1 = bf16[16,8,27,128]{3,1,2,0:T(8,128)(2,1)S(1)} async-done(((bf16[16,8,27,128]{3,1,2,0:T(8,128)(2,1)}), bf16[16,8,27,128]{3,1,2,0:T(8,128)(2,1)S(1)}, u32[]{:S(2)}, u32[]{:S(2)}) %all-to-all-start.1) | async-done | bytes 884768 | tf_op jit(solution)/shard_map/all_to_all | solution.py:46
  65.4 0.2 copy.116
  65.6 0.7 copy-done.8
  66.3 3.4 %convolution_select_fusion = f32[10,4,8,5,128]{4,2,3,1,0:T(8,128)S(1)} fusion(bf16[128,3,3,3,128]{4,0,3,2,1:T(8,128)(2,1)S(1)} %bitcast.82, bf16[10,6,1,7,2,128]{5,3,4,1,0,2:T(8,128)(2,1)S(1)} %copy-done.8, bf16[10,6,1,8,5,128]{5,3,4,1,0,2:T(8,128)(2,1)S(1)} %copy.122, pred[8,5]{0,1:T(8,128)(4,1)S(1)} %copy-done.17), kind=kOutput, calls=%fused_computation.13 | convolution fusion | flops 1323991040 | bytes 2533416 | tf_op jit(solution)/shard_map/conv_general_dilated | solution.py:26
  69.7 0.2 copy.123
  70.0 0.4 fusion.20
  70.4 0.2 slice.64
  70.6 0.3 copy-done.7
  70.9 4.6 %fusion.22 = f32[128,3,3,3,128]{4,0,3,2,1:T(8,128)S(1)} fusion(bf16[1,10,4,32,128]{4,3,2,1,0:T(8,128)(2,1)S(1)} %copy-done.7, bf16[1,10,2,32,128]{4,2,3,1,0:T(2,128)(2,1)S(1)} %slice.64), kind=kOutput, calls=%fused_computation.39 | convolution fusion | flops 517472256 | bytes 2260992 | tf_op jit(solution)/shard_map/conv_general_dilated | solution.py:33
  75.5 1.0 fusion.1
  76.5 0.3 copy.161
  76.8 5.1 %collective-permute-start.4 = (f32[16,2,4,27,128]{4,2,3,1,0:T(4,128)S(1)}, f32[16,2,4,27,128]{4,2,3,1,0:T(4,128)S(1)}, u32[]{:S(2)}, u32[]{:S(2)}) collective-permute-start(f32[16,2,4,27,128]{4,2,3,1,0:T(4,128)S(1)} %bitcast.72), channel_id=1, source_target_pairs={{0,1},{1,0},{2,3},{3,2},{4,5},{5,4},{6,7},{7,6},{8,9},{9,8},{10,11... | collective-permute-start | bytes 5308424 | tf_op jit(solution)/shard_map/ppermute | solution.py:64
  81.9 3.3 %collective-permute-done.4 = f32[16,2,4,27,128]{4,2,3,1,0:T(4,128)S(1)} collective-permute-done((f32[16,2,4,27,128]{4,2,3,1,0:T(4,128)S(1)}, f32[16,2,4,27,128]{4,2,3,1,0:T(4,128)S(1)}, u32[]{:S(2)}, u32[]{:S(2)}) %collective-permute-start.4) | collective-permute-done | bytes 1769504 | tf_op jit(solution)/shard_map/ppermute | solution.py:64
  85.2 1.4 fusion.2
  86.6 4.1 %all-to-all-start.2 = ((bf16[16,2,4,27,128]{4,2,3,1,0:T(4,128)(2,1)}), bf16[16,2,4,27,128]{4,2,3,1,0:T(4,128)(2,1)S(1)}, u32[]{:S(2)}, u32[]{:S(2)}) async-start(bf16[16,2,4,27,128]{4,2,3,1,0:T(4,128)(2,1)} %fusion.2), calls=%async_computation.2 | async-start | bytes 1769472 | tf_op jit(solution)/shard_map/all_to_all | solution.py:65
  91.1 0.4 fusion.21
  91.8 20.4 %all-to-all-done.2 = bf16[16,2,4,27,128]{4,2,3,1,0:T(4,128)(2,1)S(1)} async-done(((bf16[16,2,4,27,128]{4,2,3,1,0:T(4,128)(2,1)}), bf16[16,2,4,27,128]{4,2,3,1,0:T(4,128)(2,1)S(1)}, u32[]{:S(2)}, u32[]{:S(2)}) %all-to-all-start.2) | async-done | bytes 884768 | tf_op jit(solution)/shard_map/all_to_all | solution.py:65
  112.2 0.4 convert_reduce_fusion
  112.8 1.0 all_to_all.22
  113.8 15.3 %all-to-all-start.3 = ((f32[32,1,1728]{2,1,0:T(1,128)}), f32[32,1,1728]{2,1,0:T(1,128)S(1)}, u32[]{:S(2)}, u32[]{:S(2)}) async-start(f32[32,1,1728]{2,1,0:T(1,128)} %all_to_all.22), calls=%async_computation.3 | async-start | bytes 458752 | tf_op jit(solution)/shard_map/all_to_all | solution.py:69
  129.2 1.6 convolution_select_fusion.3
  130.8 0.2 copy.117
  131.0 0.4 fusion.45
  131.4 0.7 copy.138
  132.2 9.3 %all-to-all-done.3 = f32[32,1,1728]{2,1,0:T(1,128)S(1)} async-done(((f32[32,1,1728]{2,1,0:T(1,128)}), f32[32,1,1728]{2,1,0:T(1,128)S(1)}, u32[]{:S(2)}, u32[]{:S(2)}) %all-to-all-start.3) | async-done | bytes 221216 | tf_op jit(solution)/shard_map/all_to_all | solution.py:69
  141.5 0.5 reduce.1
  142.3 0.8 broadcast_in_dim.28
  143.1 5.4 %all-to-all-start.4 = ((f32[32,1,1728]{2,1,0:T(1,128)}), f32[32,1,1728]{2,1,0:T(1,128)S(1)}, u32[]{:S(2)}, u32[]{:S(2)}) async-start(f32[32,1,1728]{2,1,0:T(1,128)} %broadcast_in_dim.28), calls=%async_computation.4 | async-start | bytes 458752 | tf_op jit(solution)/shard_map/all_to_all | solution.py:72
  148.6 1.6 fusion.5
  150.2 0.2 copy.128
  150.5 0.7 copy.139
  151.2 9.9 %all-to-all-done.4 = f32[32,1,1728]{2,1,0:T(1,128)S(1)} async-done(((f32[32,1,1728]{2,1,0:T(1,128)}), f32[32,1,1728]{2,1,0:T(1,128)S(1)}, u32[]{:S(2)}, u32[]{:S(2)}) %all-to-all-start.4) | async-done | bytes 221216 | tf_op jit(solution)/shard_map/all_to_all | solution.py:72
  161.0 0.5 reduce.2
  161.9 0.7 copy.141
  162.6 0.7 copy.140
  (63 shorter events, 2.1 us)
Async XLA Ops:
  1.3 25.9 %copy-start.11 = (bf16[1,10,2,32,1]{3,2,1,4,0:T(2,128)(2,1)}, bf16[1,10,2,32,1]{3,2,1,4,0:T(2,128)(2,1)S(1)}, u32[]{:S(2)}) copy-start(bf16[1,10,2,32,1]{3,2,1,4,0:T(2,128)(2,1)S(1)} %get-tuple-element.9) | copy-start | bytes 3844
  3.3 23.8 %copy-start.10 = (f32[8,27,128]{2,0,1:T(8,128)S(1)}, f32[8,27,128]{2,0,1:T(8,128)}, u32[]{:S(2)}) copy-start(f32[8,27,128]{2,0,1:T(8,128)} %param.8) | copy-start | bytes 331780
  5.4 29.5 %all-to-all-start = ((bf16[16,8,27,128]{3,1,2,0:T(8,128)(2,1)}), bf16[16,8,27,128]{3,1,2,0:T(8,128)(2,1)S(1)}, u32[]{:S(2)}, u32[]{:S(2)}) async-start(bf16[16,8,27,128]{3,1,2,0:T(8,128)(2,1)} %broadcast_in_dim.10), calls=%async_computation | async-start | bytes 1769472 | tf_op jit(solution)/shard_map/all_to_all | solution.py:46
  14.1 13.3 %collective-permute-start.2 = (bf16[1,10,2,32,256]{4,3,2,1,0:T(8,128)(2,1)S(1)}, bf16[1,10,2,32,256]{4,3,2,1,0:T(8,128)(2,1)S(1)}, u32[]{:S(2)}, u32[]{:S(2)}) collective-permute-start(bf16[1,10,2,32,256]{4,3,2,1,0:T(8,128)(2,1)S(1)} %pad_maximum_fusion), channel_id=1, source_target_pairs={{0,1},{1,2},{2,3},{3,4},{4,5},{5,6},{6,7},{7,8},{8,9},{9,10},{10,1... | collective-permute-start | bytes 983048 | tf_op jit(solution)/shard_map/ppermute | solution.py:16
  18.9 8.2 %collective-permute-start.1 = (bf16[1,10,2,32,1]{3,2,1,4,0:T(2,128)(2,1)S(1)}, bf16[1,10,2,32,1]{3,2,1,4,0:T(2,128)(2,1)S(1)}, u32[]{:S(2)}, u32[]{:S(2)}) collective-permute-start(bf16[1,10,2,32,1]{3,2,1,4,0:T(2,128)(2,1)S(1)} %get-tuple-element.9), channel_id=1, source_target_pairs={{1,0},{2,1},{3,2},{4,3},{5,4},{6,5},{7,6},{8,7},{9,8},{10,9},{11,1... | collective-permute-start | bytes 3848 | tf_op jit(solution)/shard_map/ppermute | solution.py:17
  20.8 6.3 %collective-permute-start = (bf16[1,10,2,32,1]{3,2,1,4,0:T(2,128)(2,1)S(1)}, bf16[1,10,2,32,1]{3,2,1,4,0:T(2,128)(2,1)S(1)}, u32[]{:S(2)}, u32[]{:S(2)}) collective-permute-start(bf16[1,10,2,32,1]{3,2,1,4,0:T(2,128)(2,1)S(1)} %get-tuple-element.9), channel_id=1, source_target_pairs={{0,1},{1,2},{2,3},{3,4},{4,5},{5,6},{6,7},{7,8},{8,9},{9,10},{10,1... | collective-permute-start | bytes 3848 | tf_op jit(solution)/shard_map/ppermute | solution.py:16
  24.5 8.7 %collective-permute-start.3 = (bf16[1,10,2,32,256]{4,3,2,1,0:T(8,128)(2,1)S(1)}, bf16[1,10,2,32,256]{4,3,2,1,0:T(8,128)(2,1)S(1)}, u32[]{:S(2)}, u32[]{:S(2)}) collective-permute-start(bf16[1,10,2,32,256]{4,3,2,1,0:T(8,128)(2,1)S(1)} %pad_maximum_fusion), channel_id=1, source_target_pairs={{1,0},{2,1},{3,2},{4,3},{5,4},{6,5},{7,6},{8,7},{9,8},{10,9},{11,1... | collective-permute-start | bytes 983048 | tf_op jit(solution)/shard_map/ppermute | solution.py:17
  27.2 6.0 %copy-start.13 = (bf16[1,10,2,32,1]{3,2,1,4,0:T(2,128)(2,1)}, bf16[1,10,2,32,1]{3,2,1,4,0:T(2,128)(2,1)S(1)}, u32[]{:S(2)}) copy-start(bf16[1,10,2,32,1]{3,2,1,4,0:T(2,128)(2,1)S(1)} %collective-permute-done.1) | copy-start | bytes 3844
  27.2 6.0 %copy-start.15 = (bf16[1,10,2,32,1]{3,2,1,4,0:T(2,128)(2,1)}, bf16[1,10,2,32,1]{3,2,1,4,0:T(2,128)(2,1)S(1)}, u32[]{:S(2)}) copy-start(bf16[1,10,2,32,1]{3,2,1,4,0:T(2,128)(2,1)S(1)} %collective-permute-done) | copy-start | bytes 3844
  35.9 8.4 %copy-start.17 = (pred[8,5]{0,1:T(8,128)(4,1)S(1)}, pred[8,5]{0,1:T(8,128)(4,1)}, u32[]{:S(2)}) copy-start(pred[8,5]{0,1:T(8,128)(4,1)} %constant.57) | copy-start | bytes 124
  35.9 29.5 %all-to-all-start.1 = ((bf16[16,8,27,128]{3,1,2,0:T(8,128)(2,1)}), bf16[16,8,27,128]{3,1,2,0:T(8,128)(2,1)S(1)}, u32[]{:S(2)}, u32[]{:S(2)}) async-start(bf16[16,8,27,128]{3,1,2,0:T(8,128)(2,1)} %broadcast_in_dim.12), calls=%async_computation.1 | async-start | bytes 1769472 | tf_op jit(solution)/shard_map/all_to_all | solution.py:46
  44.3 3.3 %copy-start.3 = (bf16[16,8,27,128]{3,1,0,2:T(8,128)(2,1)}, bf16[16,8,27,128]{3,1,0,2:T(8,128)(2,1)S(1)}, u32[]{:S(2)}) copy-start(bf16[16,8,27,128]{3,1,0,2:T(8,128)(2,1)S(1)} %copy.112) | copy-start | bytes 2654212
  47.6 1.6 copy-start.9
  47.8 0.9 copy-start
  65.4 0.9 copy-start.8
  65.6 4.1 %copy-start.5 = (bf16[16,8,27,128]{3,1,0,2:T(8,128)(2,1)}, bf16[16,8,27,128]{3,1,0,2:T(8,128)(2,1)S(1)}, u32[]{:S(2)}) copy-start(bf16[16,8,27,128]{3,1,0,2:T(8,128)(2,1)S(1)} %copy.116) | copy-start | bytes 2654212
  69.9 1.0 copy-start.7
  70.9 4.6 %copy-start.2 = (f32[128,3,3,3,128]{4,0,3,2,1:T(8,128)S(1)}, f32[128,3,3,3,128]{4,0,3,2,1:T(8,128)}, u32[]{:S(2)}) copy-start(f32[128,3,3,3,128]{4,0,3,2,1:T(8,128)} %fusion.24) | copy-start | bytes 5308420
  76.8 8.4 %collective-permute-start.4 = (f32[16,2,4,27,128]{4,2,3,1,0:T(4,128)S(1)}, f32[16,2,4,27,128]{4,2,3,1,0:T(4,128)S(1)}, u32[]{:S(2)}, u32[]{:S(2)}) collective-permute-start(f32[16,2,4,27,128]{4,2,3,1,0:T(4,128)S(1)} %bitcast.72), channel_id=1, source_target_pairs={{0,1},{1,0},{2,3},{3,2},{4,5},{5,4},{6,7},{7,6},{8,9},{9,8},{10,11... | collective-permute-start | bytes 5308424 | tf_op jit(solution)/shard_map/ppermute | solution.py:64
  86.6 4.1 %copy-start.12 = (bf16[1,10,2,32,1]{3,2,1,4,0:T(2,128)(2,1)S(1)}, bf16[1,10,2,32,1]{3,2,1,4,0:T(2,128)(2,1)}, u32[]{:S(2)}) copy-start(bf16[1,10,2,32,1]{3,2,1,4,0:T(2,128)(2,1)} %copy-done.11) | copy-start | bytes 3844
  86.6 4.1 %copy-start.14 = (bf16[1,10,2,32,1]{3,2,1,4,0:T(2,128)(2,1)S(1)}, bf16[1,10,2,32,1]{3,2,1,4,0:T(2,128)(2,1)}, u32[]{:S(2)}) copy-start(bf16[1,10,2,32,1]{3,2,1,4,0:T(2,128)(2,1)} %copy-done.13) | copy-start | bytes 3844
  86.6 4.1 %copy-start.16 = (bf16[1,10,2,32,1]{3,2,1,4,0:T(2,128)(2,1)S(1)}, bf16[1,10,2,32,1]{3,2,1,4,0:T(2,128)(2,1)}, u32[]{:S(2)}) copy-start(bf16[1,10,2,32,1]{3,2,1,4,0:T(2,128)(2,1)} %copy-done.15) | copy-start | bytes 3844
  86.6 4.5 %copy-start.1 = (f32[10,4,8,5,128]{4,1,3,2,0:T(4,128)S(1)}, f32[10,4,8,5,128]{4,1,3,2,0:T(4,128)}, u32[]{:S(2)}) copy-start(f32[10,4,8,5,128]{4,1,3,2,0:T(4,128)} %copy-done) | copy-start | bytes 2457604
  86.6 25.6 %all-to-all-start.2 = ((bf16[16,2,4,27,128]{4,2,3,1,0:T(4,128)(2,1)}), bf16[16,2,4,27,128]{4,2,3,1,0:T(4,128)(2,1)S(1)}, u32[]{:S(2)}, u32[]{:S(2)}) async-start(bf16[16,2,4,27,128]{4,2,3,1,0:T(4,128)(2,1)} %fusion.2), calls=%async_computation.2 | async-start | bytes 1769472 | tf_op jit(solution)/shard_map/all_to_all | solution.py:65
  91.7 37.5 %copy-start.6 = (bf16[16,8,27,128]{3,1,0,2:T(8,128)(2,1)S(1)}, bf16[16,8,27,128]{3,1,0,2:T(8,128)(2,1)}, u32[]{:S(2)}) copy-start(bf16[16,8,27,128]{3,1,0,2:T(8,128)(2,1)} %copy-done.5) | copy-start | bytes 2654212
  113.8 27.7 %all-to-all-start.3 = ((f32[32,1,1728]{2,1,0:T(1,128)}), f32[32,1,1728]{2,1,0:T(1,128)S(1)}, u32[]{:S(2)}, u32[]{:S(2)}) async-start(f32[32,1,1728]{2,1,0:T(1,128)} %all_to_all.22), calls=%async_computation.3 | async-start | bytes 458752 | tf_op jit(solution)/shard_map/all_to_all | solution.py:69
  131.4 17.2 %copy-start.4 = (bf16[16,8,27,128]{3,1,0,2:T(8,128)(2,1)S(1)}, bf16[16,8,27,128]{3,1,0,2:T(8,128)(2,1)}, u32[]{:S(2)}) copy-start(bf16[16,8,27,128]{3,1,0,2:T(8,128)(2,1)} %copy-done.3) | copy-start | bytes 2654212
  143.1 17.9 %all-to-all-start.4 = ((f32[32,1,1728]{2,1,0:T(1,128)}), f32[32,1,1728]{2,1,0:T(1,128)S(1)}, u32[]{:S(2)}, u32[]{:S(2)}) async-start(f32[32,1,1728]{2,1,0:T(1,128)} %broadcast_in_dim.28), calls=%async_computation.4 | async-start | bytes 458752 | tf_op jit(solution)/shard_map/all_to_all | solution.py:72
where the time goes:
time: 164 us; the launch traced here: 163 us
  starting transfers between devices  59 us (36%)
  waiting for transfers between devices  57.4 us (35%)
  matrix products  20.2 us (12%)
  local copies, waits for them, and re-layouts  16 us (10%)
  other arithmetic  9.35 us (6%)
    all_to_all x1, waiting for transfers between devices, reduce_grads(): lax.all_to_all(mine.astype(jnp.bfloat16), 'dp', 0, 0).astype(jnp.float32)  20.4 us
    all_to_all x2, starting transfers between devices, gather_kernel(): full = lax.all_to_all(copies, 'dp', 0, 0).reshape((-1,) + local.shape[1:])  16.8 us
    all_to_all x1, starting transfers between devices, reduce_grads(): got = lax.all_to_all(spread, 'space', 0, 0).reshape(pairs, 2, -1)  15.3 us
    conv_general_dilated x2, matrix products, weight_grad(): lax.conv_general_dilated(padded, back, (1, 1, 1), 'VALID', dimension_numb...  10.3 us
    all_to_all x1, waiting for transfers between devices, reduce_grads(): full = lax.all_to_all(copies, 'space', 0, 0).reshape(pairs, 2, -1)  9.88 us
    conv_general_dilated x4, matrix products, conv(): lax.conv_general_dilated(padded, kernel, (1, 1, 1), 'VALID', dimension_nu...  9.86 us
    all_to_all x1, waiting for transfers between devices, reduce_grads(): got = lax.all_to_all(spread, 'space', 0, 0).reshape(pairs, 2, -1)  9.3 us
    all_to_all x2, waiting for transfers between devices, gather_kernel(): full = lax.all_to_all(copies, 'dp', 0, 0).reshape((-1,) + local.shape[1:])  8.78 us
  transfers between devices with their start and end apart: 10, of which 6 were waited for; matrix products, arithmetic and copies ran while one was open for 13% of the time, Pallas kernels for 0%

commit v1 on v0

--- a/solution.py
+++ b/solution.py
@@ -65,11 +65,14 @@
     owned = lax.all_to_all(mine.astype(jnp.bfloat16), "dp", 0, 0).astype(jnp.float32).sum(axis=0)
     pairs = size // 2
     pieces = owned.reshape(pairs, -1)
+    length = pieces.shape[1]
+    tiled = -(-length // 1024) * 1024
+    pieces = jnp.pad(pieces, ((0, 0), (0, tiled - length))).reshape(pairs, tiled // 128, 128)
     spread = jnp.repeat(pieces, 2, axis=0)
-    got = lax.all_to_all(spread, "space", 0, 0).reshape(pairs, 2, -1)
+    got = lax.all_to_all(spread, "space", 0, 0).reshape(pairs, 2, tiled // 128, 128)
     piece = lax.dynamic_index_in_dim(got, core, axis=1, keepdims=False).sum(axis=0)
     copies = jnp.broadcast_to(piece[None], (size,) + piece.shape)
-    full = lax.all_to_all(copies, "space", 0, 0).reshape(pairs, 2, -1)
+    full = lax.all_to_all(copies, "space", 0, 0).reshape(pairs, 2, tiled)[:, :, :length]
     halves = jnp.transpose(full, (1, 0, 2)).reshape((2,) + owned.shape)
     joined = jnp.transpose(halves, (1, 0, 2, 3, 4)).reshape((len(grads), rows) + grads[0].shape[1:])
     return [joined[i] for i in range(len(grads))]

time: 164 us -> 164 us (level)
  waiting for transfers between devices: 57.4 us -> 59.5 us
    unnamed x44 -> x46, local copies, waits for them, and re-layouts: 5.29 us -> 5.33 us
where the time goes in v1:
time: 164 us; the launch traced here: 163 us
  waiting for transfers between devices  59.5 us (36%)
  starting transfers between devices  58.8 us (36%)
  matrix products  20.2 us (12%)
  local copies, waits for them, and re-layouts  15.5 us (9%)
  other arithmetic  8.16 us (5%)
    all_to_all x1, waiting for transfers between devices, reduce_grads(): lax.all_to_all(mine.astype(jnp.bfloat16), 'dp', 0, 0).astype(jnp.float32)  21.3 us
    all_to_all x2, starting transfers between devices, gather_kernel(): full = lax.all_to_all(copies, 'dp', 0, 0).reshape((-1,) + local.shape[1:])  16.8 us
    all_to_all x1, starting transfers between devices, reduce_grads(): lax.all_to_all(spread, 'space', 0, 0).reshape(pairs, 2, tiled // 128, 128)  15.4 us
    all_to_all x1, waiting for transfers between devices, reduce_grads(): lax.all_to_all(spread, 'space', 0, 0).reshape(pairs, 2, tiled // 128, 128)  10.9 us
    conv_general_dilated x2, matrix products, weight_grad(): lax.conv_general_dilated(padded, back, (1, 1, 1), 'VALID', dimension_numb...  10.3 us
    conv_general_dilated x4, matrix products, conv(): lax.conv_general_dilated(padded, kernel, (1, 1, 1), 'VALID', dimension_nu...  9.86 us
    all_to_all x1, waiting for transfers between devices, reduce_grads(): lax.all_to_all(copies, 'space', 0, 0).reshape(pairs, 2, tiled)  9.56 us
    all_to_all x2, waiting for transfers between devices, gather_kernel(): full = lax.all_to_all(copies, 'dp', 0, 0).reshape((-1,) + local.shape[1:])  8.79 us
  transfers between devices with their start and end apart: 10, of which 6 were waited for; matrix products, arithmetic and copies ran while one was open for 13% of the time, Pallas kernels for 0%

profile of v1, /device:TPU:1, one launch (start us, length us, event | category | flops | bytes accessed | tf_op | source)
XLA Modules:
  0.0 163.4 jit_solution(3049606256874588802)
XLA Ops:
  0.6 0.7 convert_bitcast_fusion.2
  1.3 0.9 convert_element_type.64
  2.3 1.1 multiply_convert_fusion
  3.3 1.0 pad_maximum_fusion
  4.3 1.1 broadcast_in_dim.10
  5.4 8.7 %all-to-all-start = ((bf16[16,8,27,128]{3,1,2,0:T(8,128)(2,1)}), bf16[16,8,27,128]{3,1,2,0:T(8,128)(2,1)S(1)}, u32[]{:S(2)}, u32[]{:S(2)}) async-start(bf16[16,8,27,128]{3,1,2,0:T(8,128)(2,1)} %broadcast_in_dim.10), calls=%async_computation | async-start | bytes 1769472 | tf_op jit(solution)/shard_map/all_to_all | solution.py:46
  14.1 4.8 %collective-permute-start.2 = (bf16[1,10,2,32,256]{4,3,2,1,0:T(8,128)(2,1)S(1)}, bf16[1,10,2,32,256]{4,3,2,1,0:T(8,128)(2,1)S(1)}, u32[]{:S(2)}, u32[]{:S(2)}) collective-permute-start(bf16[1,10,2,32,256]{4,3,2,1,0:T(8,128)(2,1)S(1)} %pad_maximum_fusion), channel_id=1, source_target_pairs={{0,1},{1,2},{2,3},{3,4},{4,5},{5,6},{6,7},{7,8},{8,9},{9,10},{10,1... | collective-permute-start | bytes 983048 | tf_op jit(solution)/shard_map/ppermute | solution.py:16
  18.9 1.9 %collective-permute-start.1 = (bf16[1,10,2,32,1]{3,2,1,4,0:T(2,128)(2,1)S(1)}, bf16[1,10,2,32,1]{3,2,1,4,0:T(2,128)(2,1)S(1)}, u32[]{:S(2)}, u32[]{:S(2)}) collective-permute-start(bf16[1,10,2,32,1]{3,2,1,4,0:T(2,128)(2,1)S(1)} %get-tuple-element.9), channel_id=1, source_target_pairs={{1,0},{2,1},{3,2},{4,3},{5,4},{6,5},{7,6},{8,7},{9,8},{10,9},{11,1... | collective-permute-start | bytes 3848 | tf_op jit(solution)/shard_map/ppermute | solution.py:17
  20.9 3.6 %collective-permute-start = (bf16[1,10,2,32,1]{3,2,1,4,0:T(2,128)(2,1)S(1)}, bf16[1,10,2,32,1]{3,2,1,4,0:T(2,128)(2,1)S(1)}, u32[]{:S(2)}, u32[]{:S(2)}) collective-permute-start(bf16[1,10,2,32,1]{3,2,1,4,0:T(2,128)(2,1)S(1)} %get-tuple-element.9), channel_id=1, source_target_pairs={{0,1},{1,2},{2,3},{3,4},{4,5},{5,6},{6,7},{7,8},{8,9},{9,10},{10,1... | collective-permute-start | bytes 3848 | tf_op jit(solution)/shard_map/ppermute | solution.py:16
  24.5 1.9 %collective-permute-start.3 = (bf16[1,10,2,32,256]{4,3,2,1,0:T(8,128)(2,1)S(1)}, bf16[1,10,2,32,256]{4,3,2,1,0:T(8,128)(2,1)S(1)}, u32[]{:S(2)}, u32[]{:S(2)}) collective-permute-start(bf16[1,10,2,32,256]{4,3,2,1,0:T(8,128)(2,1)S(1)} %pad_maximum_fusion), channel_id=1, source_target_pairs={{1,0},{2,1},{3,2},{4,3},{5,4},{6,5},{7,6},{8,7},{9,8},{10,9},{11,1... | collective-permute-start | bytes 983048 | tf_op jit(solution)/shard_map/ppermute | solution.py:17
  26.4 0.7 slice.38
  27.5 5.7 %collective-permute-done.3 = bf16[1,10,2,32,256]{4,3,2,1,0:T(8,128)(2,1)S(1)} collective-permute-done((bf16[1,10,2,32,256]{4,3,2,1,0:T(8,128)(2,1)S(1)}, bf16[1,10,2,32,256]{4,3,2,1,0:T(8,128)(2,1)S(1)}, u32[]{:S(2)}, u32[]{:S(2)}) %collective-permute-start.3) | collective-permute-done | bytes 327712 | tf_op jit(solution)/shard_map/ppermute | solution.py:17
  33.2 0.8 slice.67
  34.1 0.3 fusion.59
  34.3 0.2 copy.184
  34.5 0.2 pad.12.clone
  34.9 1.0 broadcast_in_dim.12
  35.9 8.1 %all-to-all-start.1 = ((bf16[16,8,27,128]{3,1,2,0:T(8,128)(2,1)}), bf16[16,8,27,128]{3,1,2,0:T(8,128)(2,1)S(1)}, u32[]{:S(2)}, u32[]{:S(2)}) async-start(bf16[16,8,27,128]{3,1,2,0:T(8,128)(2,1)} %broadcast_in_dim.12), calls=%async_computation.1 | async-start | bytes 1769472 | tf_op jit(solution)/shard_map/all_to_all | solution.py:46
  44.1 0.2 copy.150
  44.3 3.3 %add_divide_fusion = (f32[10,4,8,5,128]{4,2,3,1,0:T(8,128)S(1)}, f32[10,4,8,5,128]{4,2,3,1,0:T(8,128)S(1)}, f32[10,4,8,5,128]{4,2,3,1,0:T(8,128)S(1)}) fusion(bf16[128,3,3,3,128]{4,0,3,2,1:T(8,128)(2,1)S(1)} %bitcast.85, bf16[10,6,1,7,2,128]{5,3,4,1,0,2:T(8,128)(2,1)S(1)} %slice.56, bf16[10,6,1,8,5,128]{5,3,4,1,0,2:T(8,128)(2,1)S(1)} %copy.149, ...), kind=kOutput, calls=%fused_computation.32 | convolution fusion | flops 1325424640 | bytes 4171816 | tf_op jit(solution)/shard_map/conv_general_dilated | solution.py:26
  47.6 0.2 copy.151
  47.9 0.9 copy-done
  48.8 0.4 fusion.65
  49.2 5.7 %fusion.24 = f32[128,3,3,3,128]{4,0,3,2,1:T(8,128)} fusion(bf16[1,10,4,32,128]{4,2,3,1,0:T(4,128)(2,1)S(1)} %fusion.65, bf16[1,10,2,32,128]{4,3,2,1,0:T(8,128)(2,1)S(1)} %copy-done.9), kind=kOutput, calls=%fused_computation.41 | convolution fusion | flops 517472256 | bytes 2260992 | tf_op jit(solution)/shard_map/conv_general_dilated | solution.py:33
  54.9 0.2 copy.162
  55.1 0.2 copy.163
  55.4 0.2 copy.185
  55.6 0.2 pad.16.clone
  55.8 0.8 slice.61
  56.6 8.8 %all-to-all-done.1 = bf16[16,8,27,128]{3,1,2,0:T(8,128)(2,1)S(1)} async-done(((bf16[16,8,27,128]{3,1,2,0:T(8,128)(2,1)}), bf16[16,8,27,128]{3,1,2,0:T(8,128)(2,1)S(1)}, u32[]{:S(2)}, u32[]{:S(2)}) %all-to-all-start.1) | async-done | bytes 884768 | tf_op jit(solution)/shard_map/all_to_all | solution.py:46
  65.4 0.2 copy.154
  65.7 0.7 copy-done.8
  66.3 3.4 %convolution_select_fusion = f32[10,4,8,5,128]{4,2,3,1,0:T(8,128)S(1)} fusion(bf16[128,3,3,3,128]{4,0,3,2,1:T(8,128)(2,1)S(1)} %bitcast.87, bf16[10,6,1,7,2,128]{5,3,4,1,0,2:T(8,128)(2,1)S(1)} %copy-done.8, bf16[10,6,1,8,5,128]{5,3,4,1,0,2:T(8,128)(2,1)S(1)} %copy.160, pred[8,5]{0,1:T(8,128)(4,1)S(1)} %copy-done.17), kind=kOutput, calls=%fused_computation.13 | convolution fusion | flops 1323991040 | bytes 2533416 | tf_op jit(solution)/shard_map/conv_general_dilated | solution.py:26
  69.8 0.2 copy.161
  70.0 0.4 fusion.20
  70.4 0.2 slice.68
  70.6 0.3 copy-done.7
  71.0 4.6 %fusion.22 = f32[128,3,3,3,128]{4,0,3,2,1:T(8,128)S(1)} fusion(bf16[1,10,4,32,128]{4,3,2,1,0:T(8,128)(2,1)S(1)} %copy-done.7, bf16[1,10,2,32,128]{4,2,3,1,0:T(2,128)(2,1)S(1)} %slice.68), kind=kOutput, calls=%fused_computation.39 | convolution fusion | flops 517472256 | bytes 2260992 | tf_op jit(solution)/shard_map/conv_general_dilated | solution.py:33
  75.5 1.0 fusion.1
  76.5 0.3 copy.198
  76.8 5.1 %collective-permute-start.4 = (f32[16,2,4,27,128]{4,2,3,1,0:T(4,128)S(1)}, f32[16,2,4,27,128]{4,2,3,1,0:T(4,128)S(1)}, u32[]{:S(2)}, u32[]{:S(2)}) collective-permute-start(f32[16,2,4,27,128]{4,2,3,1,0:T(4,128)S(1)} %bitcast.78), channel_id=1, source_target_pairs={{0,1},{1,0},{2,3},{3,2},{4,5},{5,4},{6,7},{7,6},{8,9},{9,8},{10,11... | collective-permute-start | bytes 5308424 | tf_op jit(solution)/shard_map/ppermute | solution.py:64
  81.9 3.3 %collective-permute-done.4 = f32[16,2,4,27,128]{4,2,3,1,0:T(4,128)S(1)} collective-permute-done((f32[16,2,4,27,128]{4,2,3,1,0:T(4,128)S(1)}, f32[16,2,4,27,128]{4,2,3,1,0:T(4,128)S(1)}, u32[]{:S(2)}, u32[]{:S(2)}) %collective-permute-start.4) | collective-permute-done | bytes 1769504 | tf_op jit(solution)/shard_map/ppermute | solution.py:64
  85.2 1.5 fusion.2
  86.7 4.1 %all-to-all-start.2 = ((bf16[16,2,4,27,128]{4,2,3,1,0:T(4,128)(2,1)}), bf16[16,2,4,27,128]{4,2,3,1,0:T(4,128)(2,1)S(1)}, u32[]{:S(2)}, u32[]{:S(2)}) async-start(bf16[16,2,4,27,128]{4,2,3,1,0:T(4,128)(2,1)} %fusion.2), calls=%async_computation.2 | async-start | bytes 1769472 | tf_op jit(solution)/shard_map/all_to_all | solution.py:65
  91.0 21.3 %all-to-all-done.2 = bf16[16,2,4,27,128]{4,2,3,1,0:T(4,128)(2,1)S(1)} async-done(((bf16[16,2,4,27,128]{4,2,3,1,0:T(4,128)(2,1)}), bf16[16,2,4,27,128]{4,2,3,1,0:T(4,128)(2,1)S(1)}, u32[]{:S(2)}, u32[]{:S(2)}) %all-to-all-start.2) | async-done | bytes 884768 | tf_op jit(solution)/shard_map/all_to_all | solution.py:65
  112.2 0.4 convert_reduce_fusion
  112.8 0.7 broadcast_in_dim.13
  113.5 15.4 %all-to-all-start.3 = ((f32[32,16,128]{2,1,0:T(8,128)}), f32[32,16,128]{2,1,0:T(8,128)S(1)}, u32[]{:S(2)}, u32[]{:S(2)}) async-start(f32[32,16,128]{2,1,0:T(8,128)} %bitcast.31), calls=%async_computation.3 | async-start | bytes 524288 | tf_op jit(solution)/shard_map/all_to_all | solution.py:72
  128.9 0.4 fusion.21
  129.3 0.1 pad.14
  129.6 1.6 convolution_select_fusion.3
  131.2 0.2 copy.155
  131.4 10.9 %all-to-all-done.3 = f32[32,16,128]{2,1,0:T(8,128)S(1)} async-done(((f32[32,16,128]{2,1,0:T(8,128)}), f32[32,16,128]{2,1,0:T(8,128)S(1)}, u32[]{:S(2)}, u32[]{:S(2)}) %all-to-all-start.3) | async-done | bytes 262176 | tf_op jit(solution)/shard_map/all_to_all | solution.py:72
  142.4 0.7 broadcast_in_dim.28
  143.1 5.0 %all-to-all-start.4 = ((f32[32,16,128]{2,1,0:T(8,128)}), f32[32,16,128]{2,1,0:T(8,128)S(1)}, u32[]{:S(2)}, u32[]{:S(2)}) async-start(f32[32,16,128]{2,1,0:T(8,128)} %broadcast_in_dim.28), calls=%async_computation.4 | async-start | bytes 524288 | tf_op jit(solution)/shard_map/all_to_all | solution.py:75
  148.1 0.4 fusion.45
  148.5 0.1 pad.18
  148.7 0.7 copy.176
  149.5 1.6 fusion.5
  151.1 0.2 copy.166
  151.4 0.7 copy.177
  152.1 9.6 %all-to-all-done.4 = f32[32,16,128]{2,1,0:T(8,128)S(1)} async-done(((f32[32,16,128]{2,1,0:T(8,128)}), f32[32,16,128]{2,1,0:T(8,128)S(1)}, u32[]{:S(2)}, u32[]{:S(2)}) %all-to-all-start.4) | async-done | bytes 262176 | tf_op jit(solution)/shard_map/all_to_all | solution.py:75
  162.0 0.7 copy.179
  162.7 0.7 copy.178
  (62 shorter events, 1.5 us)
Async XLA Ops:
  1.3 25.9 %copy-start.11 = (bf16[1,10,2,32,1]{3,2,1,4,0:T(2,128)(2,1)}, bf16[1,10,2,32,1]{3,2,1,4,0:T(2,128)(2,1)S(1)}, u32[]{:S(2)}) copy-start(bf16[1,10,2,32,1]{3,2,1,4,0:T(2,128)(2,1)S(1)} %get-tuple-element.9) | copy-start | bytes 3844
  3.3 23.8 %copy-start.10 = (f32[8,27,128]{2,0,1:T(8,128)S(1)}, f32[8,27,128]{2,0,1:T(8,128)}, u32[]{:S(2)}) copy-start(f32[8,27,128]{2,0,1:T(8,128)} %param.8) | copy-start | bytes 331780
  5.4 29.5 %all-to-all-start = ((bf16[16,8,27,128]{3,1,2,0:T(8,128)(2,1)}), bf16[16,8,27,128]{3,1,2,0:T(8,128)(2,1)S(1)}, u32[]{:S(2)}, u32[]{:S(2)}) async-start(bf16[16,8,27,128]{3,1,2,0:T(8,128)(2,1)} %broadcast_in_dim.10), calls=%async_computation | async-start | bytes 1769472 | tf_op jit(solution)/shard_map/all_to_all | solution.py:46
  14.1 13.3 %collective-permute-start.2 = (bf16[1,10,2,32,256]{4,3,2,1,0:T(8,128)(2,1)S(1)}, bf16[1,10,2,32,256]{4,3,2,1,0:T(8,128)(2,1)S(1)}, u32[]{:S(2)}, u32[]{:S(2)}) collective-permute-start(bf16[1,10,2,32,256]{4,3,2,1,0:T(8,128)(2,1)S(1)} %pad_maximum_fusion), channel_id=1, source_target_pairs={{0,1},{1,2},{2,3},{3,4},{4,5},{5,6},{6,7},{7,8},{8,9},{9,10},{10,1... | collective-permute-start | bytes 983048 | tf_op jit(solution)/shard_map/ppermute | solution.py:16
  18.9 8.2 %collective-permute-start.1 = (bf16[1,10,2,32,1]{3,2,1,4,0:T(2,128)(2,1)S(1)}, bf16[1,10,2,32,1]{3,2,1,4,0:T(2,128)(2,1)S(1)}, u32[]{:S(2)}, u32[]{:S(2)}) collective-permute-start(bf16[1,10,2,32,1]{3,2,1,4,0:T(2,128)(2,1)S(1)} %get-tuple-element.9), channel_id=1, source_target_pairs={{1,0},{2,1},{3,2},{4,3},{5,4},{6,5},{7,6},{8,7},{9,8},{10,9},{11,1... | collective-permute-start | bytes 3848 | tf_op jit(solution)/shard_map/ppermute | solution.py:17
  20.9 6.3 %collective-permute-start = (bf16[1,10,2,32,1]{3,2,1,4,0:T(2,128)(2,1)S(1)}, bf16[1,10,2,32,1]{3,2,1,4,0:T(2,128)(2,1)S(1)}, u32[]{:S(2)}, u32[]{:S(2)}) collective-permute-start(bf16[1,10,2,32,1]{3,2,1,4,0:T(2,128)(2,1)S(1)} %get-tuple-element.9), channel_id=1, source_target_pairs={{0,1},{1,2},{2,3},{3,4},{4,5},{5,6},{6,7},{7,8},{8,9},{9,10},{10,1... | collective-permute-start | bytes 3848 | tf_op jit(solution)/shard_map/ppermute | solution.py:16
  24.5 8.7 %collective-permute-start.3 = (bf16[1,10,2,32,256]{4,3,2,1,0:T(8,128)(2,1)S(1)}, bf16[1,10,2,32,256]{4,3,2,1,0:T(8,128)(2,1)S(1)}, u32[]{:S(2)}, u32[]{:S(2)}) collective-permute-start(bf16[1,10,2,32,256]{4,3,2,1,0:T(8,128)(2,1)S(1)} %pad_maximum_fusion), channel_id=1, source_target_pairs={{1,0},{2,1},{3,2},{4,3},{5,4},{6,5},{7,6},{8,7},{9,8},{10,9},{11,1... | collective-permute-start | bytes 983048 | tf_op jit(solution)/shard_map/ppermute | solution.py:17
  27.2 6.0 %copy-start.13 = (bf16[1,10,2,32,1]{3,2,1,4,0:T(2,128)(2,1)}, bf16[1,10,2,32,1]{3,2,1,4,0:T(2,128)(2,1)S(1)}, u32[]{:S(2)}) copy-start(bf16[1,10,2,32,1]{3,2,1,4,0:T(2,128)(2,1)S(1)} %collective-permute-done.1) | copy-start | bytes 3844
  27.2 6.0 %copy-start.15 = (bf16[1,10,2,32,1]{3,2,1,4,0:T(2,128)(2,1)}, bf16[1,10,2,32,1]{3,2,1,4,0:T(2,128)(2,1)S(1)}, u32[]{:S(2)}) copy-start(bf16[1,10,2,32,1]{3,2,1,4,0:T(2,128)(2,1)S(1)} %collective-permute-done) | copy-start | bytes 3844
  35.9 8.4 %copy-start.17 = (pred[8,5]{0,1:T(8,128)(4,1)S(1)}, pred[8,5]{0,1:T(8,128)(4,1)}, u32[]{:S(2)}) copy-start(pred[8,5]{0,1:T(8,128)(4,1)} %constant.60) | copy-start | bytes 124
  35.9 29.5 %all-to-all-start.1 = ((bf16[16,8,27,128]{3,1,2,0:T(8,128)(2,1)}), bf16[16,8,27,128]{3,1,2,0:T(8,128)(2,1)S(1)}, u32[]{:S(2)}, u32[]{:S(2)}) async-start(bf16[16,8,27,128]{3,1,2,0:T(8,128)(2,1)} %broadcast_in_dim.12), calls=%async_computation.1 | async-start | bytes 1769472 | tf_op jit(solution)/shard_map/all_to_all | solution.py:46
  44.3 3.3 %copy-start.3 = (bf16[16,8,27,128]{3,1,0,2:T(8,128)(2,1)}, bf16[16,8,27,128]{3,1,0,2:T(8,128)(2,1)S(1)}, u32[]{:S(2)}) copy-start(bf16[16,8,27,128]{3,1,0,2:T(8,128)(2,1)S(1)} %copy.150) | copy-start | bytes 2654212
  47.6 1.6 copy-start.9
  47.8 0.9 copy-start
  65.4 0.9 copy-start.8
  65.6 4.1 %copy-start.5 = (bf16[16,8,27,128]{3,1,0,2:T(8,128)(2,1)}, bf16[16,8,27,128]{3,1,0,2:T(8,128)(2,1)S(1)}, u32[]{:S(2)}) copy-start(bf16[16,8,27,128]{3,1,0,2:T(8,128)(2,1)S(1)} %copy.154) | copy-start | bytes 2654212
  70.0 1.0 copy-start.7
  70.9 4.6 %copy-start.2 = (f32[128,3,3,3,128]{4,0,3,2,1:T(8,128)S(1)}, f32[128,3,3,3,128]{4,0,3,2,1:T(8,128)}, u32[]{:S(2)}) copy-start(f32[128,3,3,3,128]{4,0,3,2,1:T(8,128)} %fusion.24) | copy-start | bytes 5308420
  76.8 8.4 %collective-permute-start.4 = (f32[16,2,4,27,128]{4,2,3,1,0:T(4,128)S(1)}, f32[16,2,4,27,128]{4,2,3,1,0:T(4,128)S(1)}, u32[]{:S(2)}, u32[]{:S(2)}) collective-permute-start(f32[16,2,4,27,128]{4,2,3,1,0:T(4,128)S(1)} %bitcast.78), channel_id=1, source_target_pairs={{0,1},{1,0},{2,3},{3,2},{4,5},{5,4},{6,7},{7,6},{8,9},{9,8},{10,11... | collective-permute-start | bytes 5308424 | tf_op jit(solution)/shard_map/ppermute | solution.py:64
  86.7 4.1 %copy-start.12 = (bf16[1,10,2,32,1]{3,2,1,4,0:T(2,128)(2,1)S(1)}, bf16[1,10,2,32,1]{3,2,1,4,0:T(2,128)(2,1)}, u32[]{:S(2)}) copy-start(bf16[1,10,2,32,1]{3,2,1,4,0:T(2,128)(2,1)} %copy-done.11) | copy-start | bytes 3844
  86.7 4.1 %copy-start.14 = (bf16[1,10,2,32,1]{3,2,1,4,0:T(2,128)(2,1)S(1)}, bf16[1,10,2,32,1]{3,2,1,4,0:T(2,128)(2,1)}, u32[]{:S(2)}) copy-start(bf16[1,10,2,32,1]{3,2,1,4,0:T(2,128)(2,1)} %copy-done.13) | copy-start | bytes 3844
  86.7 4.1 %copy-start.16 = (bf16[1,10,2,32,1]{3,2,1,4,0:T(2,128)(2,1)S(1)}, bf16[1,10,2,32,1]{3,2,1,4,0:T(2,128)(2,1)}, u32[]{:S(2)}) copy-start(bf16[1,10,2,32,1]{3,2,1,4,0:T(2,128)(2,1)} %copy-done.15) | copy-start | bytes 3844
  86.7 25.6 %all-to-all-start.2 = ((bf16[16,2,4,27,128]{4,2,3,1,0:T(4,128)(2,1)}), bf16[16,2,4,27,128]{4,2,3,1,0:T(4,128)(2,1)S(1)}, u32[]{:S(2)}, u32[]{:S(2)}) async-start(bf16[16,2,4,27,128]{4,2,3,1,0:T(4,128)(2,1)} %fusion.2), calls=%async_computation.2 | async-start | bytes 1769472 | tf_op jit(solution)/shard_map/all_to_all | solution.py:65
  90.8 38.1 %copy-start.1 = (f32[10,4,8,5,128]{4,1,3,2,0:T(4,128)S(1)}, f32[10,4,8,5,128]{4,1,3,2,0:T(4,128)}, u32[]{:S(2)}) copy-start(f32[10,4,8,5,128]{4,1,3,2,0:T(4,128)} %copy-done) | copy-start | bytes 2457604
  113.5 16.1 %copy-start.6 = (bf16[16,8,27,128]{3,1,0,2:T(8,128)(2,1)S(1)}, bf16[16,8,27,128]{3,1,0,2:T(8,128)(2,1)}, u32[]{:S(2)}) copy-start(bf16[16,8,27,128]{3,1,0,2:T(8,128)(2,1)} %copy-done.5) | copy-start | bytes 2654212
  113.5 28.8 %all-to-all-start.3 = ((f32[32,16,128]{2,1,0:T(8,128)}), f32[32,16,128]{2,1,0:T(8,128)S(1)}, u32[]{:S(2)}, u32[]{:S(2)}) async-start(f32[32,16,128]{2,1,0:T(8,128)} %bitcast.31), calls=%async_computation.3 | async-start | bytes 524288 | tf_op jit(solution)/shard_map/all_to_all | solution.py:72
  142.4 7.1 %copy-start.4 = (bf16[16,8,27,128]{3,1,0,2:T(8,128)(2,1)S(1)}, bf16[16,8,27,128]{3,1,0,2:T(8,128)(2,1)}, u32[]{:S(2)}) copy-start(bf16[16,8,27,128]{3,1,0,2:T(8,128)(2,1)} %copy-done.3) | copy-start | bytes 2654212
  143.1 18.6 %all-to-all-start.4 = ((f32[32,16,128]{2,1,0:T(8,128)}), f32[32,16,128]{2,1,0:T(8,128)S(1)}, u32[]{:S(2)}, u32[]{:S(2)}) async-start(f32[32,16,128]{2,1,0:T(8,128)} %broadcast_in_dim.28), calls=%async_computation.4 | async-start | bytes 524288 | tf_op jit(solution)/shard_map/all_to_all | solution.py:75

commit v2 on v1

--- a/solution.py
+++ b/solution.py
@@ -61,7 +61,8 @@
     parts = jnp.stack([g.reshape((count, 2, rows // 2) + g.shape[1:]) for g in grads], axis=1)
     keep = lax.dynamic_index_in_dim(parts, core, axis=2, keepdims=False)
     send = lax.dynamic_index_in_dim(parts, 1 - core, axis=2, keepdims=False)
-    mine = keep + lax.ppermute(send, "space", [(i, i ^ 1) for i in range(size)])
+    other = lax.ppermute(send.astype(jnp.bfloat16), "space", [(i, i ^ 1) for i in range(size)])
+    mine = keep + other.astype(jnp.float32)
     owned = lax.all_to_all(mine.astype(jnp.bfloat16), "dp", 0, 0).astype(jnp.float32).sum(axis=0)
     pairs = size // 2
     pieces = owned.reshape(pairs, -1)

time: 164 us -> 167 us (1.018)
  local copies, waits for them, and re-layouts: 15.5 us -> 20.9 us
  starting transfers between devices: 58.8 us -> 55.5 us
    unnamed x46 -> x60, local copies, waits for them, and re-layouts: 5.33 us -> 8.85 us
    ppermute x1, starting transfers between devices: 5.09 us -> 2.3 us  [reduce_grads(): lax.ppermute(send.astype(jnp.bfloat16), 'space', [(i, i ^ 1) for i in ran...]
    all_to_all x2, waiting for transfers between devices: 8.79 us -> 11.1 us  [gather_kernel(): full = lax.all_to_all(copies, 'dp', 0, 0).reshape((-1,) + local.shape[1:])]
  transfers between devices with their start and end apart: 10 -> 10, of which waited for: 6 -> 6; matrix products, arithmetic and copies ran while one was open for 13% -> 12% of each run, Pallas kernels for 0% -> 0%
where the time goes in v2:
time: 167 us; the launch traced here: 166 us
  waiting for transfers between devices  60.4 us (36%)
  starting transfers between devices  55.5 us (33%)
  local copies, waits for them, and re-layouts  20.9 us (13%)
  matrix products  19 us (11%)
  other arithmetic  9.03 us (5%)
    all_to_all x1, waiting for transfers between devices, reduce_grads(): lax.all_to_all(mine.astype(jnp.bfloat16), 'dp', 0, 0).astype(jnp.float32)  21.2 us
    all_to_all x2, starting transfers between devices, gather_kernel(): full = lax.all_to_all(copies, 'dp', 0, 0).reshape((-1,) + local.shape[1:])  16.8 us
    all_to_all x1, starting transfers between devices, reduce_grads(): lax.all_to_all(spread, 'space', 0, 0).reshape(pairs, 2, tiled // 128, 128)  14.9 us
    all_to_all x2, waiting for transfers between devices, gather_kernel(): full = lax.all_to_all(copies, 'dp', 0, 0).reshape((-1,) + local.shape[1:])  11.1 us
    all_to_all x1, waiting for transfers between devices, reduce_grads(): lax.all_to_all(spread, 'space', 0, 0).reshape(pairs, 2, tiled // 128, 128)  10.9 us
    conv_general_dilated x4, matrix products, conv(): lax.conv_general_dilated(padded, kernel, (1, 1, 1), 'VALID', dimension_nu...  9.86 us
    all_to_all x1, waiting for transfers between devices, reduce_grads(): lax.all_to_all(copies, 'space', 0, 0).reshape(pairs, 2, tiled)  9.55 us
    conv_general_dilated x2, matrix products, weight_grad(): lax.conv_general_dilated(padded, back, (1, 1, 1), 'VALID', dimension_numb...  9.15 us
  transfers between devices with their start and end apart: 10, of which 6 were waited for; matrix products, arithmetic and copies ran while one was open for 12% of the time, Pallas kernels for 0%

profile of v2, /device:TPU:1, one launch (start us, length us, event | category | flops | bytes accessed | tf_op | source)
XLA Modules:
  0.0 166.2 jit_solution(16511614201738387956)
XLA Ops:
  0.6 0.7 convert_bitcast_fusion.2
  1.3 0.9 convert_element_type.73
  2.3 1.1 multiply_convert_fusion
  3.3 1.0 pad_maximum_fusion
  4.3 1.0 broadcast_in_dim.10
  5.4 8.7 %all-to-all-start = ((bf16[16,8,27,128]{3,1,2,0:T(8,128)(2,1)}), bf16[16,8,27,128]{3,1,2,0:T(8,128)(2,1)S(1)}, u32[]{:S(2)}, u32[]{:S(2)}) async-start(bf16[16,8,27,128]{3,1,2,0:T(8,128)(2,1)} %broadcast_in_dim.10), calls=%async_computation | async-start | bytes 1769472 | tf_op jit(solution)/shard_map/all_to_all | solution.py:46
  14.1 4.8 %collective-permute-start.2 = (bf16[1,10,2,32,256]{4,3,2,1,0:T(8,128)(2,1)S(1)}, bf16[1,10,2,32,256]{4,3,2,1,0:T(8,128)(2,1)S(1)}, u32[]{:S(2)}, u32[]{:S(2)}) collective-permute-start(bf16[1,10,2,32,256]{4,3,2,1,0:T(8,128)(2,1)S(1)} %pad_maximum_fusion), channel_id=1, source_target_pairs={{0,1},{1,2},{2,3},{3,4},{4,5},{5,6},{6,7},{7,8},{8,9},{9,10},{10,1... | collective-permute-start | bytes 983048 | tf_op jit(solution)/shard_map/ppermute | solution.py:16
  18.9 1.9 %collective-permute-start.1 = (bf16[1,10,2,32,1]{3,2,1,4,0:T(2,128)(2,1)S(1)}, bf16[1,10,2,32,1]{3,2,1,4,0:T(2,128)(2,1)S(1)}, u32[]{:S(2)}, u32[]{:S(2)}) collective-permute-start(bf16[1,10,2,32,1]{3,2,1,4,0:T(2,128)(2,1)S(1)} %get-tuple-element.9), channel_id=1, source_target_pairs={{1,0},{2,1},{3,2},{4,3},{5,4},{6,5},{7,6},{8,7},{9,8},{10,9},{11,1... | collective-permute-start | bytes 3848 | tf_op jit(solution)/shard_map/ppermute | solution.py:17
  20.8 3.6 %collective-permute-start = (bf16[1,10,2,32,1]{3,2,1,4,0:T(2,128)(2,1)S(1)}, bf16[1,10,2,32,1]{3,2,1,4,0:T(2,128)(2,1)S(1)}, u32[]{:S(2)}, u32[]{:S(2)}) collective-permute-start(bf16[1,10,2,32,1]{3,2,1,4,0:T(2,128)(2,1)S(1)} %get-tuple-element.9), channel_id=1, source_target_pairs={{0,1},{1,2},{2,3},{3,4},{4,5},{5,6},{6,7},{7,8},{8,9},{9,10},{10,1... | collective-permute-start | bytes 3848 | tf_op jit(solution)/shard_map/ppermute | solution.py:16
  24.5 1.9 %collective-permute-start.3 = (bf16[1,10,2,32,256]{4,3,2,1,0:T(8,128)(2,1)S(1)}, bf16[1,10,2,32,256]{4,3,2,1,0:T(8,128)(2,1)S(1)}, u32[]{:S(2)}, u32[]{:S(2)}) collective-permute-start(bf16[1,10,2,32,256]{4,3,2,1,0:T(8,128)(2,1)S(1)} %pad_maximum_fusion), channel_id=1, source_target_pairs={{1,0},{2,1},{3,2},{4,3},{5,4},{6,5},{7,6},{8,7},{9,8},{10,9},{11,1... | collective-permute-start | bytes 983048 | tf_op jit(solution)/shard_map/ppermute | solution.py:17
  26.6 0.6 copy-done.20
  27.1 0.6 copy-done.22
  28.0 5.2 %collective-permute-done.3 = bf16[1,10,2,32,256]{4,3,2,1,0:T(8,128)(2,1)S(1)} collective-permute-done((bf16[1,10,2,32,256]{4,3,2,1,0:T(8,128)(2,1)S(1)}, bf16[1,10,2,32,256]{4,3,2,1,0:T(8,128)(2,1)S(1)}, u32[]{:S(2)}, u32[]{:S(2)}) %collective-permute-start.3) | collective-permute-done | bytes 327712 | tf_op jit(solution)/shard_map/ppermute | solution.py:17
  33.2 0.8 slice.67
  34.0 1.0 fusion.63
  35.1 0.2 copy.218
  35.3 0.2 pad.12.clone
  35.6 1.0 broadcast_in_dim.12
  36.7 8.1 %all-to-all-start.1 = ((bf16[16,8,27,128]{3,1,2,0:T(8,128)(2,1)}), bf16[16,8,27,128]{3,1,2,0:T(8,128)(2,1)S(1)}, u32[]{:S(2)}, u32[]{:S(2)}) async-start(bf16[16,8,27,128]{3,1,2,0:T(8,128)(2,1)} %broadcast_in_dim.12), calls=%async_computation.1 | async-start | bytes 1769472 | tf_op jit(solution)/shard_map/all_to_all | solution.py:46
  44.8 0.2 copy.185
  45.1 3.3 %add_divide_fusion = (f32[10,4,8,5,128]{4,2,3,1,0:T(8,128)S(1)}, f32[10,4,8,5,128]{4,2,3,1,0:T(8,128)S(1)}, f32[10,4,8,5,128]{4,2,3,1,0:T(8,128)S(1)}) fusion(bf16[128,3,3,3,128]{4,0,3,2,1:T(8,128)(2,1)S(1)} %bitcast.87, bf16[10,6,1,7,2,128]{5,3,4,1,0,2:T(8,128)(2,1)S(1)} %slice.56, bf16[10,6,1,8,5,128]{5,3,4,1,0,2:T(8,128)(2,1)S(1)} %copy.184, ...), kind=kOutput, calls=%fused_computation.34 | convolution fusion | flops 1325424640 | bytes 4171816 | tf_op jit(solution)/shard_map/conv_general_dilated | solution.py:26
  48.4 0.2 copy.186
  48.6 0.9 copy-done
  49.5 0.4 fusion.69
  49.9 4.6 %fusion.28 = f32[128,3,3,3,128]{4,0,3,2,1:T(8,128)S(1)} fusion(bf16[1,10,4,32,128]{4,2,3,1,0:T(4,128)(2,1)S(1)} %fusion.69, bf16[1,10,2,32,128]{4,3,2,1,0:T(8,128)(2,1)S(1)} %slice.38), kind=kOutput, calls=%fused_computation.43 | convolution fusion | flops 517472256 | bytes 2260992 | tf_op jit(solution)/shard_map/conv_general_dilated | solution.py:33
  54.5 0.2 copy.197
  54.7 1.1 copy.198
  55.8 0.2 copy.219
  56.3 0.8 copy-done.9
  57.1 0.8 slice.61
  57.9 11.1 %all-to-all-done.1 = bf16[16,8,27,128]{3,1,2,0:T(8,128)(2,1)S(1)} async-done(((bf16[16,8,27,128]{3,1,2,0:T(8,128)(2,1)}), bf16[16,8,27,128]{3,1,2,0:T(8,128)(2,1)S(1)}, u32[]{:S(2)}, u32[]{:S(2)}) %all-to-all-start.1) | async-done | bytes 884768 | tf_op jit(solution)/shard_map/all_to_all | solution.py:46
  69.0 0.2 copy.189
  69.3 0.9 copy-done.13
  70.2 3.4 %convolution_select_fusion = f32[10,4,8,5,128]{4,2,3,1,0:T(8,128)S(1)} fusion(bf16[128,3,3,3,128]{4,0,3,2,1:T(8,128)(2,1)S(1)} %bitcast.89, bf16[10,6,1,7,2,128]{5,3,4,1,0,2:T(8,128)(2,1)S(1)} %copy-done.16, bf16[10,6,1,8,5,128]{5,3,4,1,0,2:T(8,128)(2,1)S(1)} %copy-done.10, pred[8,5]{0,1:T(8,128)(4,1)S(1)} %copy-done.24), kind=kOutput, calls=%fused_computation.14 | convolution fusion | flops 1323991040 | bytes 2533416 | tf_op jit(solution)/shard_map/conv_general_dilated | solution.py:26
  73.6 0.2 copy.196
  73.9 0.9 copy-done.2
  74.8 0.4 fusion.24
  75.2 0.7 copy-done.6
  76.0 0.2 slice.68
  76.2 4.6 %fusion.26 = f32[128,3,3,3,128]{4,0,3,2,1:T(8,128)S(1)} fusion(bf16[1,10,4,32,128]{4,3,2,1,0:T(8,128)(2,1)S(1)} %copy-done.15, bf16[1,10,2,32,128]{4,2,3,1,0:T(2,128)(2,1)S(1)} %slice.68), kind=kOutput, calls=%fused_computation.41 | convolution fusion | flops 517472256 | bytes 2260992 | tf_op jit(solution)/shard_map/conv_general_dilated | solution.py:33
  80.7 1.4 fusion.11
  82.2 2.3 %collective-permute-start.4 = (bf16[16,2,4,27,128]{4,2,0,3,1:T(4,128)(2,1)}, bf16[16,2,4,27,128]{4,2,0,3,1:T(4,128)(2,1)}, u32[]{:S(2)}, u32[]{:S(2)}) collective-permute-start(bf16[16,2,4,27,128]{4,2,0,3,1:T(4,128)(2,1)} %fusion.11), channel_id=1, source_target_pairs={{0,1},{1,0},{2,3},{3,2},{4,5},{5,4},{6,7},{7,6},{8,9},{9,8},{10,11... | collective-permute-start | bytes 2654216 | tf_op jit(solution)/shard_map/ppermute | solution.py:64
  84.5 2.4 %collective-permute-done.4 = bf16[16,2,4,27,128]{4,2,0,3,1:T(4,128)(2,1)} collective-permute-done((bf16[16,2,4,27,128]{4,2,0,3,1:T(4,128)(2,1)}, bf16[16,2,4,27,128]{4,2,0,3,1:T(4,128)(2,1)}, u32[]{:S(2)}, u32[]{:S(2)}) %collective-permute-start.4) | collective-permute-done | bytes 884768 | tf_op jit(solution)/shard_map/ppermute | solution.py:64
  86.8 1.8 %fusion.5 = bf16[16,2,4,27,128]{4,2,0,3,1:T(4,128)(2,1)S(1)} fusion(s32[]{:T(128)S(6)} %select_n.17, f32[16,1,2,4,27,128]{5,3,2,0,4,1:T(4,128)S(1)} %bitcast.73, f32[16,1,2,4,27,128]{5,3,2,0,4,1:T(4,128)S(1)} %bitcast.71, bf16[16,2,4,27,128]{4,2,0,3,1:T(4,128)(2,1)} %collective-permute-done.4), kind=kLoop, calls=%fused_computation.9 | loop fusion | flops 1769472 | bytes 5308420 | tf_op jit(solution)/shard_map/convert_element_type | solution.py:66
  88.7 1.2 copy.205
  89.9 4.0 %all-to-all-start.2 = ((bf16[16,2,4,27,128]{4,2,3,1,0:T(4,128)(2,1)}), bf16[16,2,4,27,128]{4,2,3,1,0:T(4,128)(2,1)S(1)}, u32[]{:S(2)}, u32[]{:S(2)}) async-start(bf16[16,2,4,27,128]{4,2,3,1,0:T(4,128)(2,1)} %copy.205), calls=%async_computation.2 | async-start | bytes 1769472 | tf_op jit(solution)/shard_map/all_to_all | solution.py:66
  94.2 21.2 %all-to-all-done.2 = bf16[16,2,4,27,128]{4,2,3,1,0:T(4,128)(2,1)S(1)} async-done(((bf16[16,2,4,27,128]{4,2,3,1,0:T(4,128)(2,1)}), bf16[16,2,4,27,128]{4,2,3,1,0:T(4,128)(2,1)S(1)}, u32[]{:S(2)}, u32[]{:S(2)}) %all-to-all-start.2) | async-done | bytes 884768 | tf_op jit(solution)/shard_map/all_to_all | solution.py:66
  115.5 0.4 convert_reduce_fusion
  116.0 0.7 broadcast_in_dim.13
  116.7 14.9 %all-to-all-start.3 = ((f32[32,16,128]{2,1,0:T(8,128)}), f32[32,16,128]{2,1,0:T(8,128)S(1)}, u32[]{:S(2)}, u32[]{:S(2)}) async-start(f32[32,16,128]{2,1,0:T(8,128)} %bitcast.31), calls=%async_computation.3 | async-start | bytes 524288 | tf_op jit(solution)/shard_map/all_to_all | solution.py:73
  131.6 0.4 fusion.25
  132.3 1.6 convolution_select_fusion.3
  133.9 0.2 copy.190
  134.1 10.9 %all-to-all-done.3 = f32[32,16,128]{2,1,0:T(8,128)S(1)} async-done(((f32[32,16,128]{2,1,0:T(8,128)}), f32[32,16,128]{2,1,0:T(8,128)S(1)}, u32[]{:S(2)}, u32[]{:S(2)}) %all-to-all-start.3) | async-done | bytes 262176 | tf_op jit(solution)/shard_map/all_to_all | solution.py:73
  145.0 0.7 broadcast_in_dim.28
  145.8 5.2 %all-to-all-start.4 = ((f32[32,16,128]{2,1,0:T(8,128)}), f32[32,16,128]{2,1,0:T(8,128)S(1)}, u32[]{:S(2)}, u32[]{:S(2)}) async-start(f32[32,16,128]{2,1,0:T(8,128)} %broadcast_in_dim.28), calls=%async_computation.4 | async-start | bytes 524288 | tf_op jit(solution)/shard_map/all_to_all | solution.py:76
  150.9 0.4 fusion.49
  151.5 0.7 copy.210
  152.3 1.6 fusion.8
  153.9 0.2 copy.201
  154.2 0.7 copy.211
  154.9 9.5 %all-to-all-done.4 = f32[32,16,128]{2,1,0:T(8,128)S(1)} async-done(((f32[32,16,128]{2,1,0:T(8,128)}), f32[32,16,128]{2,1,0:T(8,128)S(1)}, u32[]{:S(2)}, u32[]{:S(2)}) %all-to-all-start.4) | async-done | bytes 262176 | tf_op jit(solution)/shard_map/all_to_all | solution.py:76
  164.8 0.7 copy.213
  165.5 0.7 copy.212
  (76 shorter events, 2.1 us)
Async XLA Ops:
  1.3 25.2 %copy-start.18 = (bf16[1,10,2,32,1]{3,2,1,4,0:T(2,128)(2,1)}, bf16[1,10,2,32,1]{3,2,1,4,0:T(2,128)(2,1)S(1)}, u32[]{:S(2)}) copy-start(bf16[1,10,2,32,1]{3,2,1,4,0:T(2,128)(2,1)S(1)} %get-tuple-element.9) | copy-start | bytes 3844
  3.3 23.2 %copy-start.17 = (f32[8,27,128]{2,0,1:T(8,128)S(1)}, f32[8,27,128]{2,0,1:T(8,128)}, u32[]{:S(2)}) copy-start(f32[8,27,128]{2,0,1:T(8,128)} %param.8) | copy-start | bytes 331780
  5.4 30.2 %all-to-all-start = ((bf16[16,8,27,128]{3,1,2,0:T(8,128)(2,1)}), bf16[16,8,27,128]{3,1,2,0:T(8,128)(2,1)S(1)}, u32[]{:S(2)}, u32[]{:S(2)}) async-start(bf16[16,8,27,128]{3,1,2,0:T(8,128)(2,1)} %broadcast_in_dim.10), calls=%async_computation | async-start | bytes 1769472 | tf_op jit(solution)/shard_map/all_to_all | solution.py:46
  14.1 13.8 %collective-permute-start.2 = (bf16[1,10,2,32,256]{4,3,2,1,0:T(8,128)(2,1)S(1)}, bf16[1,10,2,32,256]{4,3,2,1,0:T(8,128)(2,1)S(1)}, u32[]{:S(2)}, u32[]{:S(2)}) collective-permute-start(bf16[1,10,2,32,256]{4,3,2,1,0:T(8,128)(2,1)S(1)} %pad_maximum_fusion), channel_id=1, source_target_pairs={{0,1},{1,2},{2,3},{3,4},{4,5},{5,6},{6,7},{7,8},{8,9},{9,10},{10,1... | collective-permute-start | bytes 983048 | tf_op jit(solution)/shard_map/ppermute | solution.py:16
  18.9 7.6 %collective-permute-start.1 = (bf16[1,10,2,32,1]{3,2,1,4,0:T(2,128)(2,1)S(1)}, bf16[1,10,2,32,1]{3,2,1,4,0:T(2,128)(2,1)S(1)}, u32[]{:S(2)}, u32[]{:S(2)}) collective-permute-start(bf16[1,10,2,32,1]{3,2,1,4,0:T(2,128)(2,1)S(1)} %get-tuple-element.9), channel_id=1, source_target_pairs={{1,0},{2,1},{3,2},{4,3},{5,4},{6,5},{7,6},{8,7},{9,8},{10,9},{11,1... | collective-permute-start | bytes 3848 | tf_op jit(solution)/shard_map/ppermute | solution.py:17
  20.8 5.7 %collective-permute-start = (bf16[1,10,2,32,1]{3,2,1,4,0:T(2,128)(2,1)S(1)}, bf16[1,10,2,32,1]{3,2,1,4,0:T(2,128)(2,1)S(1)}, u32[]{:S(2)}, u32[]{:S(2)}) collective-permute-start(bf16[1,10,2,32,1]{3,2,1,4,0:T(2,128)(2,1)S(1)} %get-tuple-element.9), channel_id=1, source_target_pairs={{0,1},{1,2},{2,3},{3,4},{4,5},{5,6},{6,7},{7,8},{8,9},{9,10},{10,1... | collective-permute-start | bytes 3848 | tf_op jit(solution)/shard_map/ppermute | solution.py:16
  24.5 8.7 %collective-permute-start.3 = (bf16[1,10,2,32,256]{4,3,2,1,0:T(8,128)(2,1)S(1)}, bf16[1,10,2,32,256]{4,3,2,1,0:T(8,128)(2,1)S(1)}, u32[]{:S(2)}, u32[]{:S(2)}) collective-permute-start(bf16[1,10,2,32,256]{4,3,2,1,0:T(8,128)(2,1)S(1)} %pad_maximum_fusion), channel_id=1, source_target_pairs={{1,0},{2,1},{3,2},{4,3},{5,4},{6,5},{7,6},{8,7},{9,8},{10,9},{11,1... | collective-permute-start | bytes 983048 | tf_op jit(solution)/shard_map/ppermute | solution.py:17
  26.5 0.6 copy-start.20
  27.1 0.6 copy-start.22
  27.9 20.7 %copy-start.3 = (f32[10,4,32]{1,2,0:T(8,128)}, f32[10,4,32]{1,2,0:T(8,128)S(1)}, u32[]{:S(2)}) copy-start(f32[10,4,32]{1,2,0:T(8,128)S(1)} %copy.181) | copy-start | bytes 15364
  36.7 8.4 %copy-start.24 = (pred[8,5]{0,1:T(8,128)(4,1)S(1)}, pred[8,5]{0,1:T(8,128)(4,1)}, u32[]{:S(2)}) copy-start(pred[8,5]{0,1:T(8,128)(4,1)} %constant.60) | copy-start | bytes 124
  36.7 32.4 %all-to-all-start.1 = ((bf16[16,8,27,128]{3,1,2,0:T(8,128)(2,1)}), bf16[16,8,27,128]{3,1,2,0:T(8,128)(2,1)S(1)}, u32[]{:S(2)}, u32[]{:S(2)}) async-start(bf16[16,8,27,128]{3,1,2,0:T(8,128)(2,1)} %broadcast_in_dim.12), calls=%async_computation.1 | async-start | bytes 1769472 | tf_op jit(solution)/shard_map/all_to_all | solution.py:46
  45.1 3.3 %copy-start.11 = (bf16[16,8,27,128]{3,1,0,2:T(8,128)(2,1)}, bf16[16,8,27,128]{3,1,0,2:T(8,128)(2,1)S(1)}, u32[]{:S(2)}) copy-start(bf16[16,8,27,128]{3,1,0,2:T(8,128)(2,1)S(1)} %copy.185) | copy-start | bytes 2654212
  48.6 0.9 copy-start
  54.5 1.3 copy-start.8
  56.3 0.8 copy-start.9
  69.0 1.2 copy-start.10
  69.0 1.2 copy-start.16
  69.3 0.9 copy-start.13
  73.6 1.1 copy-start.2
  73.6 1.2 copy-start.4
  73.9 2.3 %copy-start.15 = (bf16[1,10,4,32,128]{4,3,2,1,0:T(8,128)(2,1)S(1)}, bf16[1,10,4,32,128]{4,3,2,1,0:T(8,128)(2,1)}, u32[]{:S(2)}) copy-start(bf16[1,10,4,32,128]{4,3,2,1,0:T(8,128)(2,1)} %slice.67) | copy-start | bytes 983044
  75.2 0.7 copy-start.6
  82.2 4.7 %collective-permute-start.4 = (bf16[16,2,4,27,128]{4,2,0,3,1:T(4,128)(2,1)}, bf16[16,2,4,27,128]{4,2,0,3,1:T(4,128)(2,1)}, u32[]{:S(2)}, u32[]{:S(2)}) collective-permute-start(bf16[16,2,4,27,128]{4,2,0,3,1:T(4,128)(2,1)} %fusion.11), channel_id=1, source_target_pairs={{0,1},{1,0},{2,3},{3,2},{4,5},{5,4},{6,7},{7,6},{8,9},{9,8},{10,11... | collective-permute-start | bytes 2654216 | tf_op jit(solution)/shard_map/ppermute | solution.py:64
  88.7 5.3 %copy-start.19 = (bf16[1,10,2,32,1]{3,2,1,4,0:T(2,128)(2,1)S(1)}, bf16[1,10,2,32,1]{3,2,1,4,0:T(2,128)(2,1)}, u32[]{:S(2)}) copy-start(bf16[1,10,2,32,1]{3,2,1,4,0:T(2,128)(2,1)} %copy-done.18) | copy-start | bytes 3844
  88.7 5.3 %copy-start.21 = (bf16[1,10,2,32,1]{3,2,1,4,0:T(2,128)(2,1)S(1)}, bf16[1,10,2,32,1]{3,2,1,4,0:T(2,128)(2,1)}, u32[]{:S(2)}) copy-start(bf16[1,10,2,32,1]{3,2,1,4,0:T(2,128)(2,1)} %copy-done.20) | copy-start | bytes 3844
  88.7 5.3 %copy-start.23 = (bf16[1,10,2,32,1]{3,2,1,4,0:T(2,128)(2,1)S(1)}, bf16[1,10,2,32,1]{3,2,1,4,0:T(2,128)(2,1)}, u32[]{:S(2)}) copy-start(bf16[1,10,2,32,1]{3,2,1,4,0:T(2,128)(2,1)} %copy-done.22) | copy-start | bytes 3844
  89.9 25.5 %all-to-all-start.2 = ((bf16[16,2,4,27,128]{4,2,3,1,0:T(4,128)(2,1)}), bf16[16,2,4,27,128]{4,2,3,1,0:T(4,128)(2,1)S(1)}, u32[]{:S(2)}, u32[]{:S(2)}) async-start(bf16[16,2,4,27,128]{4,2,3,1,0:T(4,128)(2,1)} %copy.205), calls=%async_computation.2 | async-start | bytes 1769472 | tf_op jit(solution)/shard_map/all_to_all | solution.py:66
  94.0 37.6 %copy-start.1 = (f32[10,4,8,5,128]{4,1,3,2,0:T(4,128)S(1)}, f32[10,4,8,5,128]{4,1,3,2,0:T(4,128)}, u32[]{:S(2)}) copy-start(f32[10,4,8,5,128]{4,1,3,2,0:T(4,128)} %copy-done) | copy-start | bytes 2457604
  94.0 37.6 %copy-start.5 = (f32[10,4,32]{1,2,0:T(8,128)S(1)}, f32[10,4,32]{1,2,0:T(8,128)}, u32[]{:S(2)}) copy-start(f32[10,4,32]{1,2,0:T(8,128)} %copy-done.3) | copy-start | bytes 15364
  116.7 15.6 %copy-start.14 = (bf16[16,8,27,128]{3,1,0,2:T(8,128)(2,1)S(1)}, bf16[16,8,27,128]{3,1,0,2:T(8,128)(2,1)}, u32[]{:S(2)}) copy-start(bf16[16,8,27,128]{3,1,0,2:T(8,128)(2,1)} %copy-done.13) | copy-start | bytes 2654212
  116.7 28.3 %all-to-all-start.3 = ((f32[32,16,128]{2,1,0:T(8,128)}), f32[32,16,128]{2,1,0:T(8,128)S(1)}, u32[]{:S(2)}, u32[]{:S(2)}) async-start(f32[32,16,128]{2,1,0:T(8,128)} %bitcast.31), calls=%async_computation.3 | async-start | bytes 524288 | tf_op jit(solution)/shard_map/all_to_all | solution.py:73
  133.9 17.4 %copy-start.7 = (bf16[10,4,1,32,128]{4,1,3,0,2:T(4,128)(2,1)S(1)}, bf16[10,4,1,32,128]{4,1,3,0,2:T(4,128)(2,1)}, u32[]{:S(2)}) copy-start(bf16[10,4,1,32,128]{4,1,3,0,2:T(4,128)(2,1)} %copy-done.6) | copy-start | bytes 983044
  145.8 6.5 %copy-start.12 = (bf16[16,8,27,128]{3,1,0,2:T(8,128)(2,1)S(1)}, bf16[16,8,27,128]{3,1,0,2:T(8,128)(2,1)}, u32[]{:S(2)}) copy-start(bf16[16,8,27,128]{3,1,0,2:T(8,128)(2,1)} %copy-done.11) | copy-start | bytes 2654212
  145.8 18.7 %all-to-all-start.4 = ((f32[32,16,128]{2,1,0:T(8,128)}), f32[32,16,128]{2,1,0:T(8,128)S(1)}, u32[]{:S(2)}, u32[]{:S(2)}) async-start(f32[32,16,128]{2,1,0:T(8,128)} %broadcast_in_dim.28), calls=%async_computation.4 | async-start | bytes 524288 | tf_op jit(solution)/shard_map/all_to_all | solution.py:76
